TPU v7x, 512 devices: a whole 4x4x16 slice. The times are simulated.
512 devices in a mesh: dp: 64 (over z, x_lo, core), tensor: 8 (over y, x_hi).
Axes of the slice: x: 4 (x_hi: 2, x_lo: 2; x = x_hi * 2 + x_lo), y: 4, z: 16, core: 2. Of those that a mesh axis runs over, the one named last changes fastest.
Arguments:
- hidden_in: bfloat16 [16384, 4096], P(('dp', 'tensor')), may hold values from -12 to 12
- norm_gain: bfloat16 [4096], replicated, may hold values from 0.5 to 1.5
- w_query: bfloat16 [4096, 4096], P('dp', 'tensor'), may hold values from -0.11328125 to 0.11328125
- w_key: bfloat16 [4096, 1024], P('dp', 'tensor'), may hold values from -0.11328125 to 0.11328125
- w_value: bfloat16 [4096, 1024], P('dp', 'tensor'), may hold values from -0.09375 to 0.09375
- w_out: bfloat16 [4096, 4096], P('tensor', 'dp'), may hold values from -0.09375 to 0.09375
- segment: int32 [16384], P('dp'), may hold values from -1 to 1, as said below
Outputs:
- hidden_out: bfloat16 [16384, 4096], P(('dp', 'tensor'))
- kv_cache: bfloat16 [16384, 8, 256], P('dp', 'tensor')
Inputs may be any that keep to these rules, and one draw needn't show every extreme that they name: `segment`: within each pack of 256 rows, prompts are numbered from 0 in order and each starts at a multiple of 128; a prompt's last tile may end in rows of -1, and whole tiles of -1 may only follow the last prompt of a pack; the first tile of every pack holds a prompt; in every draw some pack has no tile of -1 only and holds one prompt a tile.
All inputs are finite; a program needn't handle non-finite values.
Results may differ from a plain program's by a relative error of at most 0.0085.
Values may be sent and summed in bfloat16 or wider, within the bound.
No kernel may reach another device: no remote copies, remote signals or barrier semaphores. Data moves between devices by JAX's collectives and lax.ppermute only.
A program may use at most 64 MiB of HBM per device.

v0:
```python
import jax
import jax.numpy as jnp
from jax import lax
from jax.sharding import PartitionSpec as P

HEAD = 128
rope_theta = 500000.0
norm_epsilon = 1e-05


def inverse_frequency(head_width):
    exponent = jnp.arange(0, head_width, 2).astype(jnp.float32) / head_width
    base_freq = rope_theta ** (-exponent)
    wavelength = 2.0 * jnp.pi / base_freq
    smooth = (8192.0 / wavelength - 1.0) / 3.0
    blended = (1.0 - smooth) * base_freq / 8.0 + smooth * base_freq
    return jnp.where(
        wavelength < 2048.0, base_freq, jnp.where(wavelength > 8192.0, base_freq / 8.0, blended)
    )


def positions_of(segment):
    row_index = jnp.arange(segment.shape[0], dtype=jnp.int32)
    changed = jnp.concatenate([jnp.ones((1,), dtype=bool), segment[1:] != segment[:-1]])
    begins = lax.cummax(jnp.where(changed, row_index, 0), axis=0)
    return row_index - begins


def rotate(vectors, position):
    head_width = vectors.shape[-1]
    half_width = head_width // 2
    angles = position.astype(jnp.float32)[:, None] * inverse_frequency(head_width)[None, :]
    cosine = jnp.concatenate([jnp.cos(angles), jnp.cos(angles)], axis=-1)[:, None, :]
    sine_table = jnp.concatenate([jnp.sin(angles), jnp.sin(angles)], axis=-1)[:, None, :]
    turned = jnp.concatenate([-vectors[..., half_width:], vectors[..., :half_width]], axis=-1)
    return vectors * cosine + turned * sine_table


def rms_normed(rows_float, norm_gain):
    mean_square = jnp.mean(rows_float * rows_float, axis=-1, keepdims=True)
    return (
        rows_float * lax.rsqrt(mean_square + norm_epsilon) * norm_gain.astype(jnp.float32)
    ).astype(jnp.bfloat16)


def visible_pairs(segment, key_count):
    row_index = jnp.arange(segment.shape[0], dtype=jnp.int32)
    key_index = jnp.arange(key_count, dtype=jnp.int32)
    same_segment = (segment[:, None] == segment[None, :]) & (segment[:, None] >= 0)
    causal = key_index[None, :] <= row_index[:, None]
    return same_segment & causal | (key_index[None, :] == row_index[:, None])


def body(hidden_in, norm_gain, w_query, w_key, w_value, w_out, segment):
    pack_rows = segment.shape[0]
    query_cols = w_query.shape[1]
    kv_cols = w_key.shape[1]
    query_heads = query_cols // HEAD
    kv_heads = kv_cols // HEAD
    group_size = query_heads // kv_heads
    score_scale = HEAD ** (-0.5)
    rows_float = hidden_in.astype(jnp.float32)
    normed = rms_normed(rows_float, norm_gain)
    tensor_size = pack_rows // normed.shape[0]
    gathered = lax.all_to_all(
        jnp.broadcast_to(normed[None], (tensor_size,) + normed.shape), "tensor", 0, 0, tiled=True
    ).reshape(pack_rows, normed.shape[1])
    packed = jnp.concatenate((w_query, w_key, w_value, w_out.T), axis=1)
    packed_full = lax.all_gather(packed, "dp", axis=0, tiled=True)
    joined = packed_full[:, : query_cols + 2 * kv_cols]
    out_full_t = packed_full[:, query_cols + 2 * kv_cols :]
    projected = jnp.dot(gathered, joined, preferred_element_type=jnp.float32)
    position = positions_of(segment)
    query_rows = rotate(
        projected[:, :query_cols].reshape(pack_rows, query_heads, HEAD), position
    ).astype(jnp.bfloat16)
    key_rows = rotate(
        projected[:, query_cols : query_cols + kv_cols].reshape(pack_rows, kv_heads, HEAD), position
    ).astype(jnp.bfloat16)
    value_rows = (
        projected[:, query_cols + kv_cols :].astype(jnp.bfloat16).reshape(pack_rows, kv_heads, HEAD)
    )
    cache_rows = jnp.concatenate([key_rows, value_rows], axis=-1)
    grouped_query = query_rows.reshape(pack_rows, kv_heads, group_size, HEAD)
    scores = (
        jnp.einsum("skgh,tkh->kgst", grouped_query, key_rows, preferred_element_type=jnp.float32)
        * score_scale
    )
    allowed = visible_pairs(segment, pack_rows)
    scores = jnp.where(allowed, scores, -1e30)
    row_max = jnp.max(scores, axis=-1, keepdims=True)
    weight = jnp.exp(scores - row_max)
    weight_sum = jnp.sum(weight, axis=-1)
    mixed_rows = (
        jnp.einsum(
            "kgst,tkh->kgsh",
            weight.astype(jnp.bfloat16),
            value_rows,
            preferred_element_type=jnp.float32,
        )
        / weight_sum[..., None]
    )
    attended = (
        jnp.transpose(mixed_rows, (2, 0, 1, 3)).astype(jnp.bfloat16).reshape(pack_rows, query_cols)
    )
    out_rows = lax.dot_general(
        attended, out_full_t, (((1,), (1,)), ((), ())), preferred_element_type=jnp.float32
    )
    pieces = lax.all_to_all(
        out_rows.astype(jnp.bfloat16).reshape(tensor_size, -1, out_rows.shape[1]),
        "tensor",
        0,
        0,
        tiled=True,
    )
    summed = jnp.sum(pieces.astype(jnp.float32), axis=0)
    hidden_out = (summed + rows_float).astype(jnp.bfloat16)
    return (hidden_out, cache_rows)


def solution(mesh):
    return jax.shard_map(
        body,
        mesh=mesh,
        in_specs=(
            P(("dp", "tensor"), None),
            P(),
            P("dp", "tensor"),
            P("dp", "tensor"),
            P("dp", "tensor"),
            P("tensor", "dp"),
            P("dp"),
        ),
        out_specs=(P(("dp", "tensor"), None), P("dp", "tensor", None)),
        check_vma=False,
    )
```

profile of v0, /device:TPU:1, one launch (start us, length us, event | category | flops | bytes accessed | tf_op | source)
XLA Modules:
  0.0 200.9 jit_solution(4414675054207526265)
XLA Ops:
  7.2 0.0 copy-start.1
  7.2 0.0 all-gather.2.cloned.1.call-start
  7.2 1.6 pad_maximum_fusion
  8.8 0.0 all-gather.2.cloned.1.call-update
  8.8 0.7 convert_element_type.62
  9.5 1.1 fusion.8
  10.7 1.1 fusion.10
  11.7 1.5 broadcast_in_dim.13
  13.3 7.5 %all-to-all-start = ((bf16[8,32,4096]{2,1,0:T(8,128)(2,1)}), bf16[8,32,4096]{2,1,0:T(8,128)(2,1)S(1)}, u32[]{:S(2)}, u32[]{:S(2)}) async-start(bf16[8,32,4096]{2,1,0:T(8,128)(2,1)} %broadcast_in_dim.13), calls=%async_computation | async-start | bytes 4194304 | tf_op jit(solution)/shard_map/all_to_all | solution.py:65
  20.7 0.0 copy-done.1
  20.8 0.1 slice_compare_fusion
  20.8 0.1 fusion.27
  20.9 0.3 reduce-window.9
  21.2 0.1 slice.45
  21.4 0.1 slice_reduce_fusion
  21.5 0.1 fusion.28
  21.6 0.1 fusion.20
  21.7 0.5 multiply_cosine_fusion
  22.2 31.2 %all-to-all-done = bf16[8,32,4096]{2,1,0:T(8,128)(2,1)S(1)} async-done(((bf16[8,32,4096]{2,1,0:T(8,128)(2,1)}), bf16[8,32,4096]{2,1,0:T(8,128)(2,1)S(1)}, u32[]{:S(2)}, u32[]{:S(2)}) %all-to-all-start) | async-done | bytes 2097184 | tf_op jit(solution)/shard_map/all_to_all | solution.py:65
  53.4 94.2 %all-gather.2.cloned.1.call-done = bf16[4096,1280]{1,0:T(8,128)(2,1)} async-done(((bf16[64,1280]{1,0:T(8,128)(2,1)}), bf16[4096,1280]{1,0:T(8,128)(2,1)}) %all-gather.2.cloned.1.call-update) | async-done | bytes 10485776 | tf_op jit(solution)/shard_map/all_gather | solution.py:69
  147.6 4.6 %fusion = f32[256,768]{1,0:T(8,128)S(1)} fusion(bf16[256,4096]{1,0:T(8,128)(2,1)S(1)} %bitcast.71, bf16[4096,1280]{1,0:T(8,128)(2,1)} %all-gather.2.cloned.1.call-done), kind=kOutput, calls=%fused_computation | convolution fusion | flops 1610612736 | bytes 9175040 | tf_op jit(solution)/shard_map/dot_general | solution.py:72
  152.2 0.1 slice.58
  152.3 0.1 fusion.21
  152.4 0.2 reshape.137
  152.6 0.3 slice_negate_fusion
  152.9 0.2 fusion.23
  153.1 0.4 maximum_multiply_fusion
  153.5 0.1 mul.123
  153.6 0.4 fusion.29
  153.9 0.2 fusion.6
  154.1 0.3 fusion.5
  154.4 4.8 %convolution_convert_fusion = bf16[256,4096]{1,0:T(8,128)(2,1)} fusion(bf16[256,512]{0,1:T(8,128)(2,1)S(1)} %bitcast.77, bf16[4096,1280]{1,0:T(8,128)(2,1)} %all-gather.2.cloned.1.call-done), kind=kOutput, calls=%fused_computation.2 | convolution fusion | flops 1074790400 | bytes 6553600 | tf_op jit(solution)/shard_map/dot_general | solution.py:106
  159.2 0.0 copy-start
  159.2 5.8 %all-to-all-start.1 = ((bf16[8,32,4096]{2,1,0:T(8,128)(2,1)}), bf16[8,32,4096]{2,1,0:T(8,128)(2,1)S(1)}, u32[]{:S(2)}, u32[]{:S(2)}) async-start(bf16[8,32,4096]{2,1,0:T(8,128)(2,1)} %bitcast.72), calls=%async_computation.1 | async-start | bytes 4194304 | tf_op jit(solution)/shard_map/all_to_all | solution.py:109
  165.0 0.7 pad_maximum_fusion.3
  165.7 27.3 %all-to-all-done.1 = bf16[8,32,4096]{2,1,0:T(8,128)(2,1)S(1)} async-done(((bf16[8,32,4096]{2,1,0:T(8,128)(2,1)}), bf16[8,32,4096]{2,1,0:T(8,128)(2,1)S(1)}, u32[]{:S(2)}, u32[]{:S(2)}) %all-to-all-start.1) | async-done | bytes 2097184 | tf_op jit(solution)/shard_map/all_to_all | solution.py:109
  193.0 0.3 convert_reduce_fusion
  193.3 0.0 copy-done
  193.3 0.8 fusion.11
  (6 shorter events, 0.1 us)
Async XLA Ops:
  7.2 13.6 %copy-start.1 = (s32[256]{0:T(256)S(1)}, s32[256]{0:T(256)}, u32[]{:S(2)}) copy-start(s32[256]{0:T(256)} %param.13) | copy-start | bytes 3076
  7.2 140.5 %all-gather.2.cloned.1.call-start = ((), (), s32[]{:S(2)}) async-start(), calls=%async_computation.2 | async-start | bytes 10649600 | tf_op jit(solution)/shard_map/all_gather | solution.py:69
  13.3 40.1 %all-to-all-start = ((bf16[8,32,4096]{2,1,0:T(8,128)(2,1)}), bf16[8,32,4096]{2,1,0:T(8,128)(2,1)S(1)}, u32[]{:S(2)}, u32[]{:S(2)}) async-start(bf16[8,32,4096]{2,1,0:T(8,128)(2,1)} %broadcast_in_dim.13), calls=%async_computation | async-start | bytes 4194304 | tf_op jit(solution)/shard_map/all_to_all | solution.py:65
  159.2 34.0 %copy-start = (bf16[32,4096]{1,0:T(8,128)(2,1)S(1)}, bf16[32,4096]{1,0:T(8,128)(2,1)}, u32[]{:S(2)}) copy-start(bf16[32,4096]{1,0:T(8,128)(2,1)} %param.7) | copy-start | bytes 786436
  159.2 33.7 %all-to-all-start.1 = ((bf16[8,32,4096]{2,1,0:T(8,128)(2,1)}), bf16[8,32,4096]{2,1,0:T(8,128)(2,1)S(1)}, u32[]{:S(2)}, u32[]{:S(2)}) async-start(bf16[8,32,4096]{2,1,0:T(8,128)(2,1)} %bitcast.72), calls=%async_computation.1 | async-start | bytes 4194304 | tf_op jit(solution)/shard_map/all_to_all | solution.py:109
Sparse Core Ops, SparseCore 0:
  10.7 136.8 all-gather.1
where the time goes:
time: 201 us
  waiting for transfers between devices  153 us (76%)
  between operations  14.2 us (7%)
  starting transfers between devices  13.3 us (7%)
  matrix products  10 us (5%)
  other arithmetic  8.59 us (4%)
  local copies, waits for them, and re-layouts  2.09 us (1%)
    all_gather x1, waiting for transfers between devices, body(): packed_full = lax.all_gather(packed, 'dp', axis=0, tiled=True)  94.2 us
    all_to_all x1, waiting for transfers between devices, body(): lax.all_to_all(jnp.broadcast_to(normed[None], (tensor_size,) + normed.sha...  31.2 us
    all_to_all x1, waiting for transfers between devices, body(): lax.all_to_all(out_rows.astype(jnp.bfloat16).reshape(tensor_size, -1, out...  27.3 us
    all_to_all x1, starting transfers between devices, body(): lax.all_to_all(jnp.broadcast_to(normed[None], (tensor_size,) + normed.sha...  7.47 us
    all_to_all x1, starting transfers between devices, body(): lax.all_to_all(out_rows.astype(jnp.bfloat16).reshape(tensor_size, -1, out...  5.77 us
    dot_general x1, matrix products, body(): lax.dot_general(attended, out_full_t, (((1,), (1,)), ((), ())), preferred...  4.8 us
    dot_general x1, matrix products, body(): projected = jnp.dot(gathered, joined, preferred_element_type=jnp.float32)  4.56 us
  transfers between devices with their start and end apart: 3, of which 3 were waited for; matrix products, arithmetic and copies ran while one was open for 3% of the time, Pallas kernels for 0%

commit v1 on v0

--- a/solution.py
+++ b/solution.py
@@ -66,7 +66,9 @@
         jnp.broadcast_to(normed[None], (tensor_size,) + normed.shape), "tensor", 0, 0, tiled=True
     ).reshape(pack_rows, normed.shape[1])
     packed = jnp.concatenate((w_query, w_key, w_value, w_out.T), axis=1)
-    packed_full = lax.all_gather(packed, "dp", axis=0, tiled=True)
+    packed_full = jnp.concatenate(
+        lax.all_to_all(jnp.stack([packed] * lax.axis_size("dp")), "dp", 0, 0), axis=0
+    )
     joined = packed_full[:, : query_cols + 2 * kv_cols]
     out_full_t = packed_full[:, query_cols + 2 * kv_cols :]
     projected = jnp.dot(gathered, joined, preferred_element_type=jnp.float32)

time: 201 us -> 566 us (2.82)
  the two profiles are of different devices: /device:TPU:1 before, /device:TPU:34 now
where the time goes in v1:
time: 566 us; the launch traced here: 565 us
  waiting for transfers between devices  513 us (91%)
  starting transfers between devices  26.7 us (5%)
  matrix products  10 us (2%)
  local copies, waits for them, and re-layouts  7.26 us (1%)
  other arithmetic  7.07 us (1%)
    all_to_all x1, waiting for transfers between devices, body(): lax.all_to_all(jnp.stack([packed] * lax.axis_size('dp')), 'dp', 0, 0)  457 us
    all_to_all x1, waiting for transfers between devices, body(): lax.all_to_all(jnp.broadcast_to(normed[None], (tensor_size,) + normed.sha...  28.4 us
    all_to_all x1, waiting for transfers between devices, body(): lax.all_to_all(out_rows.astype(jnp.bfloat16).reshape(tensor_size, -1, out...  28.2 us
    all_to_all x1, starting transfers between devices, body(): lax.all_to_all(jnp.stack([packed] * lax.axis_size('dp')), 'dp', 0, 0)  17 us
  transfers between devices with their start and end apart: 3, of which 3 were waited for; matrix products, arithmetic and copies ran while one was open for 0% of the time, Pallas kernels for 0%

profile of v1, /device:TPU:34, one launch (start us, length us, event | category | flops | bytes accessed | tf_op | source)
XLA Modules:
  0.0 565.1 jit_solution(8455094510142542437)
XLA Ops:
  0.6 0.0 copy-start.1
  0.6 0.0 copy-start.4
  0.7 0.0 copy-start.3
  0.7 0.0 copy-start.2
  0.7 0.7 convert_element_type.62
  1.4 1.1 fusion.8
  2.5 1.1 fusion.10
  3.6 1.6 broadcast_in_dim.13
  5.2 6.0 %all-to-all-start = ((bf16[8,32,4096]{2,1,0:T(8,128)(2,1)}), bf16[8,32,4096]{2,1,0:T(8,128)(2,1)S(1)}, u32[]{:S(2)}, u32[]{:S(2)}) async-start(bf16[8,32,4096]{2,1,0:T(8,128)(2,1)} %broadcast_in_dim.13), calls=%async_computation | async-start | bytes 4194304 | tf_op jit(solution)/shard_map/all_to_all | solution.py:65
  11.3 0.0 copy-done.1
  11.3 0.0 copy-done.4
  11.3 0.0 copy-done.3
  11.3 0.0 copy-done.2
  11.3 28.4 %all-to-all-done = bf16[8,32,4096]{2,1,0:T(8,128)(2,1)S(1)} async-done(((bf16[8,32,4096]{2,1,0:T(8,128)(2,1)}), bf16[8,32,4096]{2,1,0:T(8,128)(2,1)S(1)}, u32[]{:S(2)}, u32[]{:S(2)}) %all-to-all-start) | async-done | bytes 2097184 | tf_op jit(solution)/shard_map/all_to_all | solution.py:65
  39.7 5.1 stack.2
  44.8 0.0 copy-start.5
  44.8 17.0 %all-to-all-start.1 = ((bf16[64,64,1280]{2,1,0:T(8,128)(2,1)}), bf16[64,64,1280]{2,1,0:T(8,128)(2,1)}, u32[]{:S(2)}, u32[]{:S(2)}) async-start(bf16[64,64,1280]{2,1,0:T(8,128)(2,1)} %stack.2), calls=%async_computation.1 | async-start | bytes 20971520 | tf_op jit(solution)/shard_map/all_to_all | solution.py:70
  61.8 0.0 copy-done.5
  61.8 0.1 slice_compare_fusion
  61.9 0.1 fusion.27
  62.0 0.3 reduce-window.9
  62.3 0.1 slice.45
  62.4 0.1 slice_reduce_fusion
  62.5 0.1 fusion.28
  62.6 0.1 fusion.20
  62.7 0.5 multiply_cosine_fusion
  63.3 456.6 %all-to-all-done.1 = bf16[64,64,1280]{2,1,0:T(8,128)(2,1)} async-done(((bf16[64,64,1280]{2,1,0:T(8,128)(2,1)}), bf16[64,64,1280]{2,1,0:T(8,128)(2,1)}, u32[]{:S(2)}, u32[]{:S(2)}) %all-to-all-start.1) | async-done | bytes 10485792 | tf_op jit(solution)/shard_map/all_to_all | solution.py:70
  519.9 4.6 fusion
  524.5 0.1 slice.58
  524.5 0.1 fusion.21
  524.7 0.2 reshape.143
  524.9 0.3 slice_negate_fusion
  525.2 0.2 fusion.23
  525.4 0.4 maximum_multiply_fusion
  525.7 0.1 mul.123
  525.8 0.3 fusion.29
  526.2 0.2 fusion.6
  526.3 0.3 fusion.5
  526.7 4.8 convolution_convert_fusion
  531.5 0.0 copy-start
  531.5 3.7 all-to-all-start.2
  535.2 0.7 pad_maximum_fusion.3
  535.9 28.2 %all-to-all-done.2 = bf16[8,32,4096]{2,1,0:T(8,128)(2,1)S(1)} async-done(((bf16[8,32,4096]{2,1,0:T(8,128)(2,1)}), bf16[8,32,4096]{2,1,0:T(8,128)(2,1)S(1)}, u32[]{:S(2)}, u32[]{:S(2)}) %all-to-all-start.2) | async-done | bytes 2097184 | tf_op jit(solution)/shard_map/all_to_all | solution.py:111
  564.1 0.3 convert_reduce_fusion
  564.4 0.0 copy-done
  564.4 0.8 fusion.11
  (7 shorter events, 0.1 us)
Async XLA Ops:
  0.6 10.6 %copy-start.1 = (bf16[512,64]{0,1:T(8,128)(2,1)S(1)}, bf16[512,64]{0,1:T(8,128)(2,1)}, u32[]{:S(2)}) copy-start(bf16[512,64]{0,1:T(8,128)(2,1)} %param.12) | copy-start | bytes 196612
  0.6 10.6 %copy-start.4 = (bf16[64,128]{1,0:T(8,128)(2,1)S(1)}, bf16[64,128]{1,0:T(8,128)(2,1)}, u32[]{:S(2)}) copy-start(bf16[64,128]{1,0:T(8,128)(2,1)} %param.10) | copy-start | bytes 49156
  0.7 10.6 %copy-start.3 = (bf16[64,128]{1,0:T(8,128)(2,1)S(1)}, bf16[64,128]{1,0:T(8,128)(2,1)}, u32[]{:S(2)}) copy-start(bf16[64,128]{1,0:T(8,128)(2,1)} %param.11) | copy-start | bytes 49156
  0.7 10.6 %copy-start.2 = (bf16[64,512]{1,0:T(8,128)(2,1)S(1)}, bf16[64,512]{1,0:T(8,128)(2,1)}, u32[]{:S(2)}) copy-start(bf16[64,512]{1,0:T(8,128)(2,1)} %param.9) | copy-start | bytes 196612
  5.2 34.5 %all-to-all-start = ((bf16[8,32,4096]{2,1,0:T(8,128)(2,1)}), bf16[8,32,4096]{2,1,0:T(8,128)(2,1)S(1)}, u32[]{:S(2)}, u32[]{:S(2)}) async-start(bf16[8,32,4096]{2,1,0:T(8,128)(2,1)} %broadcast_in_dim.13), calls=%async_computation | async-start | bytes 4194304 | tf_op jit(solution)/shard_map/all_to_all | solution.py:65
  44.8 17.0 %copy-start.5 = (s32[256]{0:T(256)S(1)}, s32[256]{0:T(256)}, u32[]{:S(2)}) copy-start(s32[256]{0:T(256)} %param.13) | copy-start | bytes 3076
  44.8 475.1 %all-to-all-start.1 = ((bf16[64,64,1280]{2,1,0:T(8,128)(2,1)}), bf16[64,64,1280]{2,1,0:T(8,128)(2,1)}, u32[]{:S(2)}, u32[]{:S(2)}) async-start(bf16[64,64,1280]{2,1,0:T(8,128)(2,1)} %stack.2), calls=%async_computation.1 | async-start | bytes 20971520 | tf_op jit(solution)/shard_map/all_to_all | solution.py:70
  531.5 32.9 %copy-start = (bf16[32,4096]{1,0:T(8,128)(2,1)S(1)}, bf16[32,4096]{1,0:T(8,128)(2,1)}, u32[]{:S(2)}) copy-start(bf16[32,4096]{1,0:T(8,128)(2,1)} %param.7) | copy-start | bytes 786436
  531.5 32.6 %all-to-all-start.2 = ((bf16[8,32,4096]{2,1,0:T(8,128)(2,1)}), bf16[8,32,4096]{2,1,0:T(8,128)(2,1)S(1)}, u32[]{:S(2)}, u32[]{:S(2)}) async-start(bf16[8,32,4096]{2,1,0:T(8,128)(2,1)} %bitcast.73), calls=%async_computation.2 | async-start | bytes 4194304 | tf_op jit(solution)/shard_map/all_to_all | solution.py:111
